TPU v7x, 32 devices: a whole 2x2x4 slice. The times are simulated.
32 devices in a mesh: req: 8 (over y, x, core), head: 4 (over z).
Axes of the slice: x: 2, y: 2, z: 4, core: 2. Of those that a mesh axis runs over, the one named last changes fastest.
Arguments:
- queries: bfloat16 [4096, 8192], P('req', 'head'), may hold values from -150 to 150, as said below
- new_keys: bfloat16 [4096, 1024], P('req', 'head'), may hold values from -6 to 6, as said below
- fresh_values: bfloat16 [4096, 1024], P('req', 'head'), may hold values from -6 to 6
- key_page_pool: bfloat16 [224, 128, 1024], P('req', None, 'head'), may hold values from -6 to 6
- value_page_pool: bfloat16 [224, 128, 1024], P('req', None, 'head'), may hold values from -6 to 6
- page_table: int32 [16, 14], P('req'), may hold values from 0 to 27, as said below
- new_counts: int32 [16], P('req'), may hold values from 1 to 256, 2048 in all
- cached_lens: int32 [16], P('req'), may hold values from 1 to 1536, 8192 in all
- deal_offset: int32 [8], P('req'), may hold values from 0 to 7
- residual: bfloat16 [2112, 8192], P('req', 'head'), may hold values from -1.1953125 to 1.1953125
- out_weight: bfloat16 [8192, 8192], P('head', 'req'), may hold values from -0.09375 to 0.09375
Outputs:
- hidden: bfloat16 [2112, 8192], P('req', 'head')
- keys_out: bfloat16 [224, 128, 1024], P('req', None, 'head')
- values_out: bfloat16 [224, 128, 1024], P('req', None, 'head')
Inputs may be any that keep to these rules, and one draw needn't show every extreme that they name: `new_counts`: the counts sum to 2048; the largest is exactly 256. `cached_lens`: the counts sum to 8192; the largest is exactly 1536. `page_table`: the 2 rows of each aligned block of requests hold together each of 0 to 27 once. `queries`: real values. `new_keys`: real values.
All inputs are finite; a program needn't handle non-finite values. No bound on the sum of `new_counts` or of `cached_lens` on one device may be relied on, other than what follows from the above.
Results may differ from a plain program's by a relative error of at most 0.0085.
Values may be sent and summed in bfloat16 or wider, within the bound.
No kernel may reach another device: no remote copies, remote signals or barrier semaphores. Data moves between devices by JAX's collectives and lax.ppermute only.
A program may use at most 128 MiB of HBM per device.

v0:
```python
import math
import jax
import jax.numpy as jnp
from jax import lax
from jax.sharding import PartitionSpec as P

HEAD_SIZE = 128
NEGATIVE = -1e30


def head_attention(query_matrix, prior_keys, prior_values, visible, scale_factor):
    scores = (
        jnp.einsum("tkd,skd->kts", query_matrix, prior_keys, preferred_element_type=jnp.float32)
        * scale_factor
    )
    spots_all = jnp.arange(prior_keys.shape[0], dtype=jnp.int32)
    allowed = spots_all[None, None, :] <= visible[None, :, None]
    scores = jnp.where(allowed, scores, NEGATIVE)
    highest = jnp.max(scores, axis=2, keepdims=True)
    expo_terms = jnp.where(allowed, jnp.exp(scores - highest), 0.0)
    weights = (expo_terms / jnp.sum(expo_terms, axis=2, keepdims=True)).astype(jnp.bfloat16)
    mixed = jnp.einsum("kts,skd->tkd", weights, prior_values, preferred_element_type=jnp.float32)
    return mixed.astype(jnp.bfloat16)


def deal(row_block, new_counts, lead_in, shares, starts, totals, balanced):
    groups = lax.axis_size("req")
    my_rank = lax.axis_index("req")
    per_group = new_counts.shape[0]
    new_limit = row_block.shape[0] // per_group
    pair_slots = row_block.shape[0] // groups
    columns = row_block.shape[1]
    own_lead = lax.dynamic_index_in_dim(lead_in, my_rank, 0, keepdims=False)
    ordinal = jnp.arange(pair_slots, dtype=jnp.int32)[None, :] * groups + own_lead[:, None]
    ends_at = jnp.cumsum(new_counts)
    request_index = jnp.sum(
        (ordinal[:, :, None] >= ends_at[None, None, :]).astype(jnp.int32), axis=2
    )
    request_index = jnp.minimum(request_index, per_group - 1)
    before = ends_at - new_counts
    source = request_index * new_limit + ordinal - jnp.take(before, request_index)
    own_total = lax.dynamic_index_in_dim(totals, my_rank, 0, keepdims=False)
    is_live = ordinal < own_total
    source = jnp.where(is_live, source, 0)
    picked = jnp.take(row_block, source.reshape(-1), axis=0).reshape(groups, pair_slots, columns)
    outgoing = jnp.where(is_live[:, :, None], picked, jnp.zeros((), row_block.dtype))
    arrived = lax.all_to_all(outgoing, "req", split_axis=0, concat_axis=0, tiled=True)
    own_shares = lax.dynamic_index_in_dim(shares, my_rank, 1, keepdims=False)
    own_starts = lax.dynamic_index_in_dim(starts, my_rank, 1, keepdims=False)
    within = jnp.arange(pair_slots, dtype=jnp.int32)[None, :]
    landing = jnp.where(within < own_shares[:, None], own_starts[:, None] + within, balanced)
    blank_rows = jnp.zeros((balanced, columns), row_block.dtype)
    return blank_rows.at[landing.reshape(-1)].set(arrived.reshape(-1, columns), mode="drop")


def project(row_block, out_weight):
    return jnp.dot(
        row_block,
        lax.all_gather(out_weight, "req", axis=1, tiled=True),
        preferred_element_type=jnp.float32,
    )


def head_total(partial_sum):
    return lax.psum_scatter(
        partial_sum.astype(jnp.bfloat16), "head", scatter_dimension=1, tiled=True
    ).astype(jnp.float32)


def local(
    queries,
    new_keys,
    fresh_values,
    key_page_pool,
    value_page_pool,
    page_table,
    new_counts,
    cached_lens,
    deal_offset,
    residual,
    out_weight,
):
    groups = lax.axis_size("req")
    per_group = new_counts.shape[0]
    page_count = page_table.shape[1]
    page_rows = key_page_pool.shape[1]
    channel_count = key_page_pool.shape[2]
    kv_local = channel_count // HEAD_SIZE
    slot_count = queries.shape[0]
    new_limit = slot_count // per_group
    q_width = queries.shape[1]
    group_fanout = q_width // channel_count
    balanced = residual.shape[0]
    new_slot = jnp.arange(new_limit, dtype=jnp.int32)
    positions = cached_lens[:, None] + new_slot[None, :]
    page_of = jnp.take_along_axis(page_table, positions // page_rows, axis=1)
    outside = key_page_pool.shape[0] * page_rows
    target = jnp.where(
        new_slot[None, :] < new_counts[:, None],
        page_of * page_rows + positions % page_rows,
        outside,
    ).reshape(-1)
    flat_keys = key_page_pool.reshape(-1, channel_count).at[target].set(new_keys, mode="drop")
    flat_values = (
        value_page_pool.reshape(-1, channel_count).at[target].set(fresh_values, mode="drop")
    )
    gathered_keys = flat_keys.reshape(key_page_pool.shape)
    gathered_values = flat_values.reshape(value_page_pool.shape)
    scale_factor = 1.0 / math.sqrt(HEAD_SIZE)
    pieces = []
    for member in range(per_group):
        prior_keys = gathered_keys[page_table[member]].reshape(
            page_count * page_rows, kv_local, HEAD_SIZE
        )
        prior_values = gathered_values[page_table[member]].reshape(
            page_count * page_rows, kv_local, HEAD_SIZE
        )
        query_matrix = queries[member * new_limit : (member + 1) * new_limit].reshape(
            new_limit, kv_local, group_fanout, HEAD_SIZE
        )
        query_matrix = jnp.moveaxis(query_matrix, 2, 0)
        visible = positions[member]
        mixed = lax.map(
            lambda single: head_attention(single, prior_keys, prior_values, visible, scale_factor),
            query_matrix,
        )
        pieces.append(jnp.moveaxis(mixed, 0, 2).reshape(new_limit, q_width))
    attended = jnp.concatenate(pieces, axis=0)
    load_counts, offsets_all = (
        lax.all_gather(new_counts, "req", axis=0, tiled=True),
        lax.all_gather(deal_offset, "req", axis=0, tiled=True),
    )
    totals = jnp.sum(load_counts.reshape(groups, per_group), axis=1)
    rank_ids = jnp.arange(groups, dtype=jnp.int32)
    lead_in = jnp.remainder(rank_ids[None, :] - offsets_all[:, None], groups)
    shares = jnp.maximum((totals[:, None] - lead_in + groups - 1) // groups, 0)
    starts = jnp.cumsum(shares, axis=0) - shares
    summed = head_total(project(attended, out_weight)).astype(jnp.bfloat16)
    placed = deal(summed, new_counts, lead_in, shares, starts, totals, balanced)
    hidden = (residual.astype(jnp.float32) + placed.astype(jnp.float32)).astype(jnp.bfloat16)
    return (hidden, gathered_keys, gathered_values)


def solution(mesh):
    placed = (
        P("req", "head"),
        P("req", "head"),
        P("req", "head"),
        P("req", None, "head"),
        P("req", None, "head"),
        P("req", None),
        P("req"),
        P("req"),
        P("req"),
        P("req", "head"),
        P("head", "req"),
    )
    return jax.shard_map(
        local,
        mesh=mesh,
        in_specs=placed,
        out_specs=(P("req", "head"), P("req", None, "head"), P("req", None, "head")),
        check_vma=False,
    )
```

profile of v0, /device:TPU:0, one launch (start us, length us, event | category | flops | bytes accessed | tf_op | source)
XLA Modules:
  0.0 404.9 jit_solution(16835856660951470666)
XLA Ops:
  7.2 2.9 copy.77
  11.1 4.7 %gather_fusion.6 = s32[512]{0:T(512)S(1)} fusion(s32[2,14]{1,0:T(2,128)S(1)} %copy-done, s32[512]{0:T(512)S(1)} %bitcast.125), kind=kCustom, calls=%fused_computation.6 | custom fusion | bytes 8192 | tf_op jit(solution)/shard_map/jit(take_along_axis)/gather | solution.py:96
  15.9 5.5 %scatter_fusion = bf16[3584,256]{1,0:T(8,128)(2,1)} fusion(bf16[3584,256]{1,0:T(8,128)(2,1)} %bitcast.130, s32[512]{0:T(512)S(1)} %bitcast.143, bf16[512,256]{1,0:T(8,128)(2,1)S(1)} %copy-done.7), kind=kCustom, calls=%fused_computation.7 | custom fusion | bytes 788480 | tf_op jit(solution)/shard_map/scatter | solution.py:103
  21.4 3.5 gather_fusion.3
  25.0 3.6 scatter_fusion.1
  30.1 3.1 gather_fusion.1
  48.2 66.8 %while.21 = (s32[]{:T(128)}, bf16[8,256,2,128]{1,3,0,2:T(8,128)(2,1)S(1)}, s32[1,256]{1,0:T(1,128)S(1)}, bf16[8,256,2,128]{1,3,0,2:T(8,128)(2,1)}, bf16[1792,2,1...) while((s32[]{:T(128)}, bf16[8,256,2,128]{1,3,0,2:T(8,128)(2,1)S(1)}, ...), condition=%wide.region_13.14_spmd, body=%wide.region_10.13_spmd.sunk | while | flops 476710656 | bytes 11342941 | solution.py:123
  48.5 4.6 %fusion.93 = (f32[2,256]{1,0:T(2,128)S(1)}, f32[2,256,1792]{2,1,0:T(8,128)}) fusion(bf16[1792,2,128]{2,0,1:T(8,128)(2,1)S(1)} %get-tuple-element.251, pred[256,1792]{1,0:T(8,128)(4,1)S(1)} %iota_compare_fusion.6, bf16[8,256,2,128]{1,3,0,2:T(8,128)(2,1)} %get-tuple-element.250, s32[]{:T(128)S(6)} %copy.63), kind=kOutput, calls=%fused_computation.132.clone.1 | convolution fusion | flops 239470336 | bytes 5638148 | tf_op jit(solution)/shard_map/while/body/eval_jaxpr/sub | solution.py:20
  53.1 3.0 fusion.94
  56.6 4.6 %fusion.93 = (f32[2,256]{1,0:T(2,128)S(1)}, f32[2,256,1792]{2,1,0:T(8,128)}) fusion(bf16[1792,2,128]{2,0,1:T(8,128)(2,1)S(1)} %get-tuple-element.251, pred[256,1792]{1,0:T(8,128)(4,1)S(1)} %iota_compare_fusion.6, bf16[8,256,2,128]{1,3,0,2:T(8,128)(2,1)} %get-tuple-element.250, s32[]{:T(128)S(6)} %copy.63), kind=kOutput, calls=%fused_computation.132.clone.1 | convolution fusion | flops 239470336 | bytes 5638148 | tf_op jit(solution)/shard_map/while/body/eval_jaxpr/sub | solution.py:20
  61.3 3.0 fusion.94
  64.7 4.6 %fusion.93 = (f32[2,256]{1,0:T(2,128)S(1)}, f32[2,256,1792]{2,1,0:T(8,128)}) fusion(bf16[1792,2,128]{2,0,1:T(8,128)(2,1)S(1)} %get-tuple-element.251, pred[256,1792]{1,0:T(8,128)(4,1)S(1)} %iota_compare_fusion.6, bf16[8,256,2,128]{1,3,0,2:T(8,128)(2,1)} %get-tuple-element.250, s32[]{:T(128)S(6)} %copy.63), kind=kOutput, calls=%fused_computation.132.clone.1 | convolution fusion | flops 239470336 | bytes 5638148 | tf_op jit(solution)/shard_map/while/body/eval_jaxpr/sub | solution.py:20
  69.4 3.0 fusion.94
  72.8 4.6 %fusion.93 = (f32[2,256]{1,0:T(2,128)S(1)}, f32[2,256,1792]{2,1,0:T(8,128)}) fusion(bf16[1792,2,128]{2,0,1:T(8,128)(2,1)S(1)} %get-tuple-element.251, pred[256,1792]{1,0:T(8,128)(4,1)S(1)} %iota_compare_fusion.6, bf16[8,256,2,128]{1,3,0,2:T(8,128)(2,1)} %get-tuple-element.250, s32[]{:T(128)S(6)} %copy.63), kind=kOutput, calls=%fused_computation.132.clone.1 | convolution fusion | flops 239470336 | bytes 5638148 | tf_op jit(solution)/shard_map/while/body/eval_jaxpr/sub | solution.py:20
  77.5 4.4 %fusion.94 = bf16[1,256,2,128]{3,1,2,0:T(8,128)(2,1)S(1)} fusion(bf16[1792,2,128]{2,0,1:T(8,128)(2,1)} %get-tuple-element.252, f32[2,256,1792]{2,1,0:T(8,128)} %get-tuple-element.231, f32[2,256]{1,0:T(2,128)S(1)} %get-tuple-element.232), kind=kOutput, calls=%fused_computation.37.clone.1 | convolution fusion | flops 236781568 | bytes 4720640 | tf_op jit(solution)/shard_map/while/body/eval_jaxpr/kts,skd->tkd/dot_general | solution.py:22
  82.3 4.7 %fusion.93 = (f32[2,256]{1,0:T(2,128)S(1)}, f32[2,256,1792]{2,1,0:T(8,128)}) fusion(bf16[1792,2,128]{2,0,1:T(8,128)(2,1)S(1)} %get-tuple-element.251, pred[256,1792]{1,0:T(8,128)(4,1)S(1)} %iota_compare_fusion.6, bf16[8,256,2,128]{1,3,0,2:T(8,128)(2,1)} %get-tuple-element.250, s32[]{:T(128)S(6)} %copy.63), kind=kOutput, calls=%fused_computation.132.clone.1 | convolution fusion | flops 239470336 | bytes 5638148 | tf_op jit(solution)/shard_map/while/body/eval_jaxpr/sub | solution.py:20
  87.0 3.0 fusion.94
  90.5 4.6 %fusion.93 = (f32[2,256]{1,0:T(2,128)S(1)}, f32[2,256,1792]{2,1,0:T(8,128)}) fusion(bf16[1792,2,128]{2,0,1:T(8,128)(2,1)S(1)} %get-tuple-element.251, pred[256,1792]{1,0:T(8,128)(4,1)S(1)} %iota_compare_fusion.6, bf16[8,256,2,128]{1,3,0,2:T(8,128)(2,1)} %get-tuple-element.250, s32[]{:T(128)S(6)} %copy.63), kind=kOutput, calls=%fused_computation.132.clone.1 | convolution fusion | flops 239470336 | bytes 5638148 | tf_op jit(solution)/shard_map/while/body/eval_jaxpr/sub | solution.py:20
  95.1 3.0 fusion.94
  98.6 4.6 %fusion.93 = (f32[2,256]{1,0:T(2,128)S(1)}, f32[2,256,1792]{2,1,0:T(8,128)}) fusion(bf16[1792,2,128]{2,0,1:T(8,128)(2,1)S(1)} %get-tuple-element.251, pred[256,1792]{1,0:T(8,128)(4,1)S(1)} %iota_compare_fusion.6, bf16[8,256,2,128]{1,3,0,2:T(8,128)(2,1)} %get-tuple-element.250, s32[]{:T(128)S(6)} %copy.63), kind=kOutput, calls=%fused_computation.132.clone.1 | convolution fusion | flops 239470336 | bytes 5638148 | tf_op jit(solution)/shard_map/while/body/eval_jaxpr/sub | solution.py:20
  103.2 3.5 fusion.94
  107.2 4.6 %fusion.93 = (f32[2,256]{1,0:T(2,128)S(1)}, f32[2,256,1792]{2,1,0:T(8,128)}) fusion(bf16[1792,2,128]{2,0,1:T(8,128)(2,1)S(1)} %get-tuple-element.251, pred[256,1792]{1,0:T(8,128)(4,1)S(1)} %iota_compare_fusion.6, bf16[8,256,2,128]{1,3,0,2:T(8,128)(2,1)} %get-tuple-element.250, s32[]{:T(128)S(6)} %copy.63), kind=kOutput, calls=%fused_computation.132.clone.1 | convolution fusion | flops 239470336 | bytes 5638148 | tf_op jit(solution)/shard_map/while/body/eval_jaxpr/sub | solution.py:20
  111.9 3.0 fusion.94
  115.1 65.1 %while.20 = (s32[]{:T(128)}, bf16[8,256,2,128]{1,3,0,2:T(8,128)(2,1)S(1)}, s32[1,256]{1,0:T(1,128)S(1)}, bf16[8,256,2,128]{1,3,0,2:T(8,128)(2,1)}, bf16[1792,2,1...) while((s32[]{:T(128)}, bf16[8,256,2,128]{1,3,0,2:T(8,128)(2,1)S(1)}, ...), condition=%wide.region_9.10_spmd, body=%wide.region_6.9_spmd.sunk | while | flops 476710656 | bytes 11342941 | solution.py:123
  115.5 4.6 %fusion.88 = (f32[2,256]{1,0:T(2,128)S(1)}, f32[2,256,1792]{2,1,0:T(8,128)}) fusion(bf16[1792,2,128]{2,0,1:T(8,128)(2,1)S(1)} %get-tuple-element.272, pred[256,1792]{1,0:T(8,128)(4,1)S(1)} %iota_compare_fusion.5, bf16[8,256,2,128]{1,3,0,2:T(8,128)(2,1)} %get-tuple-element.271, s32[]{:T(128)S(6)} %copy.69), kind=kOutput, calls=%fused_computation.131.clone.1 | convolution fusion | flops 239470336 | bytes 5638148 | tf_op jit(solution)/shard_map/while/body/eval_jaxpr/sub | solution.py:20
  120.1 3.0 fusion.89
  123.6 4.6 %fusion.88 = (f32[2,256]{1,0:T(2,128)S(1)}, f32[2,256,1792]{2,1,0:T(8,128)}) fusion(bf16[1792,2,128]{2,0,1:T(8,128)(2,1)S(1)} %get-tuple-element.272, pred[256,1792]{1,0:T(8,128)(4,1)S(1)} %iota_compare_fusion.5, bf16[8,256,2,128]{1,3,0,2:T(8,128)(2,1)} %get-tuple-element.271, s32[]{:T(128)S(6)} %copy.69), kind=kOutput, calls=%fused_computation.131.clone.1 | convolution fusion | flops 239470336 | bytes 5638148 | tf_op jit(solution)/shard_map/while/body/eval_jaxpr/sub | solution.py:20
  128.2 3.0 fusion.89
  131.7 4.6 %fusion.88 = (f32[2,256]{1,0:T(2,128)S(1)}, f32[2,256,1792]{2,1,0:T(8,128)}) fusion(bf16[1792,2,128]{2,0,1:T(8,128)(2,1)S(1)} %get-tuple-element.272, pred[256,1792]{1,0:T(8,128)(4,1)S(1)} %iota_compare_fusion.5, bf16[8,256,2,128]{1,3,0,2:T(8,128)(2,1)} %get-tuple-element.271, s32[]{:T(128)S(6)} %copy.69), kind=kOutput, calls=%fused_computation.131.clone.1 | convolution fusion | flops 239470336 | bytes 5638148 | tf_op jit(solution)/shard_map/while/body/eval_jaxpr/sub | solution.py:20
  136.3 3.2 fusion.89
  140.0 4.6 %fusion.88 = (f32[2,256]{1,0:T(2,128)S(1)}, f32[2,256,1792]{2,1,0:T(8,128)}) fusion(bf16[1792,2,128]{2,0,1:T(8,128)(2,1)S(1)} %get-tuple-element.272, pred[256,1792]{1,0:T(8,128)(4,1)S(1)} %iota_compare_fusion.5, bf16[8,256,2,128]{1,3,0,2:T(8,128)(2,1)} %get-tuple-element.271, s32[]{:T(128)S(6)} %copy.69), kind=kOutput, calls=%fused_computation.131.clone.1 | convolution fusion | flops 239470336 | bytes 5638148 | tf_op jit(solution)/shard_map/while/body/eval_jaxpr/sub | solution.py:20
  144.6 3.0 fusion.89
  148.1 4.6 %fusion.88 = (f32[2,256]{1,0:T(2,128)S(1)}, f32[2,256,1792]{2,1,0:T(8,128)}) fusion(bf16[1792,2,128]{2,0,1:T(8,128)(2,1)S(1)} %get-tuple-element.272, pred[256,1792]{1,0:T(8,128)(4,1)S(1)} %iota_compare_fusion.5, bf16[8,256,2,128]{1,3,0,2:T(8,128)(2,1)} %get-tuple-element.271, s32[]{:T(128)S(6)} %copy.69), kind=kOutput, calls=%fused_computation.131.clone.1 | convolution fusion | flops 239470336 | bytes 5638148 | tf_op jit(solution)/shard_map/while/body/eval_jaxpr/sub | solution.py:20
  152.7 3.0 fusion.89
  156.2 4.6 %fusion.88 = (f32[2,256]{1,0:T(2,128)S(1)}, f32[2,256,1792]{2,1,0:T(8,128)}) fusion(bf16[1792,2,128]{2,0,1:T(8,128)(2,1)S(1)} %get-tuple-element.272, pred[256,1792]{1,0:T(8,128)(4,1)S(1)} %iota_compare_fusion.5, bf16[8,256,2,128]{1,3,0,2:T(8,128)(2,1)} %get-tuple-element.271, s32[]{:T(128)S(6)} %copy.69), kind=kOutput, calls=%fused_computation.131.clone.1 | convolution fusion | flops 239470336 | bytes 5638148 | tf_op jit(solution)/shard_map/while/body/eval_jaxpr/sub | solution.py:20
  160.8 3.0 fusion.89
  164.3 4.6 %fusion.88 = (f32[2,256]{1,0:T(2,128)S(1)}, f32[2,256,1792]{2,1,0:T(8,128)}) fusion(bf16[1792,2,128]{2,0,1:T(8,128)(2,1)S(1)} %get-tuple-element.272, pred[256,1792]{1,0:T(8,128)(4,1)S(1)} %iota_compare_fusion.5, bf16[8,256,2,128]{1,3,0,2:T(8,128)(2,1)} %get-tuple-element.271, s32[]{:T(128)S(6)} %copy.69), kind=kOutput, calls=%fused_computation.131.clone.1 | convolution fusion | flops 239470336 | bytes 5638148 | tf_op jit(solution)/shard_map/while/body/eval_jaxpr/sub | solution.py:20
  168.9 3.0 fusion.89
  172.4 4.6 %fusion.88 = (f32[2,256]{1,0:T(2,128)S(1)}, f32[2,256,1792]{2,1,0:T(8,128)}) fusion(bf16[1792,2,128]{2,0,1:T(8,128)(2,1)S(1)} %get-tuple-element.272, pred[256,1792]{1,0:T(8,128)(4,1)S(1)} %iota_compare_fusion.5, bf16[8,256,2,128]{1,3,0,2:T(8,128)(2,1)} %get-tuple-element.271, s32[]{:T(128)S(6)} %copy.69), kind=kOutput, calls=%fused_computation.131.clone.1 | convolution fusion | flops 239470336 | bytes 5638148 | tf_op jit(solution)/shard_map/while/body/eval_jaxpr/sub | solution.py:20
  177.0 3.0 fusion.89
  180.2 25.9 %convolution_convert_fusion = bf16[512,8192]{1,0:T(8,128)(2,1)} fusion(bf16[2048,8192]{1,0:T(8,128)(2,1)} %all-gather.2.cloned.1.call-done, bf16[256,2048]{0,1:T(8,128)(2,1)S(1)} %bitcast.138, bf16[256,2048]{0,1:T(8,128)(2,1)S(1)} %bitcast.139), kind=kOutput, calls=%fused_computation.48 | convolution fusion | flops 17188257792 | bytes 44040192 | tf_op jit(solution)/shard_map/dot_general | solution.py:57
  209.1 9.2 %all-reduce.2 = (s32[16]{0:T(128)S(1)}, s32[8]{0:T(128)S(1)}) all-reduce(s32[16]{0:T(128)S(1)} %dynamic-update-slice, s32[8]{0:T(128)S(1)} %dynamic-update-slice.1), channel_id=1, replica_groups=mesh['req'=8,'head'=4] {'req'}, use_global_device_ids=true, to_apply=%add | all-reduce | flops 24 | bytes 192
  219.8 3.6 gather_fusion
  224.9 128.4 %reduce-scatter.2.cloned.1.call-done = bf16[512,2048]{1,0:T(8,128)(2,1)} async-done(((bf16[512,8192]{1,0:T(8,128)(2,1)}), bf16[512,2048]{1,0:T(8,128)(2,1)}) %reduce-scatter.2.cloned.1.call-update) | async-done | bytes 2097168 | tf_op jit(solution)/shard_map/reduce_scatter | solution.py:65
  353.4 6.3 %gather_fusion.5 = bf16[512,2048]{1,0:T(8,128)(2,1)S(1)} fusion(bf16[512,2048]{1,0:T(8,128)(2,1)} %reduce-scatter.2.cloned.1.call-done, s32[1024]{0:T(1024)S(1)} %pad_clamp_fusion), kind=kCustom, calls=%fused_computation.5 | custom fusion | bytes 4196352 | tf_op jit(solution)/shard_map/jit(_take)/gather | solution.py:45
  361.4 3.6 all-to-all-start
  365.4 26.2 %all-to-all-done = bf16[8,64,2048]{2,1,0:T(8,128)(2,1)S(1)} async-done(((bf16[8,64,2048]{2,1,0:T(8,128)(2,1)}), bf16[8,64,2048]{2,1,0:T(8,128)(2,1)S(1)}, u32[]{:S(2)}, u32[]{:S(2)}) %all-to-all-start) | async-done | bytes 2097184 | tf_op jit(solution)/shard_map/all_to_all | solution.py:47
  391.6 3.8 scatter_custom_fusion.2
  (139 shorter events, 34.2 us)
Async XLA Ops:
  7.2 173.0 %all-gather.2.cloned.1.call-start = ((), (), s32[]{:S(2)}) async-start(), calls=%async_computation.2 | async-start | bytes 37748736 | tf_op jit(solution)/shard_map/all_gather | solution.py:59
  10.1 0.7 copy-start.9
  10.1 0.9 copy-start.10
  10.1 0.9 copy-start
  10.2 5.7 %copy-start.7 = (bf16[512,256]{1,0:T(8,128)(2,1)S(1)}, bf16[512,256]{1,0:T(8,128)(2,1)}, u32[]{:S(2)}) copy-start(bf16[512,256]{1,0:T(8,128)(2,1)} %param.16) | copy-start | bytes 786436
  10.2 343.2 %reduce-scatter.2.cloned.1.call-start = ((), (), s32[]{:S(2)}) async-start(), calls=%async_computation.3 | async-start | bytes 10485760 | tf_op jit(solution)/shard_map/reduce_scatter | solution.py:65
  15.9 9.1 %copy-start.2 = (bf16[28,128,256]{2,1,0:T(8,128)(2,1)S(1)}, bf16[28,128,256]{2,1,0:T(8,128)(2,1)}, u32[]{:S(2)}) copy-start(bf16[28,128,256]{2,1,0:T(8,128)(2,1)} %param.19) | copy-start | bytes 5505028
  15.9 9.1 %copy-start.8 = (bf16[512,256]{1,0:T(8,128)(2,1)S(1)}, bf16[512,256]{1,0:T(8,128)(2,1)}, u32[]{:S(2)}) copy-start(bf16[512,256]{1,0:T(8,128)(2,1)} %param.17) | copy-start | bytes 786436
  28.5 6.2 %copy-start.1 = (bf16[3584,256]{1,0:T(8,128)(2,1)}, bf16[3584,256]{1,0:T(8,128)(2,1)S(1)}, u32[]{:S(2)}) copy-start(bf16[3584,256]{1,0:T(8,128)(2,1)S(1)} %scatter_fusion.1) | copy-start | bytes 5505028
  37.4 2.4 copy-start.4
  40.0 1.5 copy-start.5
  44.1 2.4 copy-start.3
  46.7 1.5 copy-start.6
  206.1 0.7 copy-start.11
  361.4 30.3 %all-to-all-start = ((bf16[8,64,2048]{2,1,0:T(8,128)(2,1)}), bf16[8,64,2048]{2,1,0:T(8,128)(2,1)S(1)}, u32[]{:S(2)}, u32[]{:S(2)}) async-start(bf16[8,64,2048]{2,1,0:T(8,128)(2,1)} %select_select_fusion), calls=%async_computation.1 | async-start | bytes 4194304 | tf_op jit(solution)/shard_map/all_to_all | solution.py:47
Sparse Core Ops, SparseCore 0:
  10.3 163.3 all-gather.1
  206.3 147.0 reduce-scatter.1
where the time goes:
time: 406 us; the launch traced here: 405 us
  waiting for transfers between devices  155 us (38%)
  matrix products  150 us (37%)
  local copies, waits for them, and re-layouts  59.2 us (15%)
  between operations  15.6 us (4%)
  other arithmetic  11.8 us (3%)
  blocking collectives  9.17 us (2%)
    reduce_scatter x1, waiting for transfers between devices, head_total(): lax.psum_scatter(partial_sum.astype(jnp.bfloat16), 'head', scatter_dimens...  128 us
    sub x16, matrix products, head_attention(): expo_terms = jnp.where(allowed, jnp.exp(scores - highest), 0.0)  74.1 us
    dot_general x16, matrix products, head_attention(): jnp.einsum('kts,skd->tkd', weights, prior_values, preferred_element_type=...  49.8 us
    all_to_all x1, waiting for transfers between devices, deal(): lax.all_to_all(outgoing, 'req', split_axis=0, concat_axis=0, tiled=True)  26.2 us
    dot_general x1, matrix products, project(): jnp.dot(row_block, lax.all_gather(out_weight, 'req', axis=1, tiled=True),...  25.9 us
    unnamed x40, local copies, waits for them, and re-layouts  9.63 us
    unnamed x1, blocking collectives  9.17 us
  transfers between devices with their start and end apart: 3, of which 2 were waited for; matrix products, arithmetic and copies ran while one was open for 44% of the time, Pallas kernels for 0%

commit v1 on v0

--- a/solution.py
+++ b/solution.py
@@ -1,3 +1,4 @@
+import functools
 import math
 import jax
 import jax.numpy as jnp
@@ -6,6 +7,25 @@
 
 HEAD_SIZE = 128
 NEGATIVE = -1e30
+
+
+def proceed_islands(xs, ax_name):
+    side_arr, y2 = (lax.axis_size(ax_name), lax.axis_index(ax_name))
+    arr_next = xs.shape[0] // side_arr
+    n_now = jnp.roll(xs, shift=-y2 * arr_next, axis=0)
+    stack_in = [lax.slice_in_dim(n_now, 0, arr_next, axis=0)]
+    for m in range(1, side_arr):
+        odd = lax.slice_in_dim(n_now, m * arr_next, (m + 1) * arr_next, axis=0)
+        stack_in.append(
+            lax.ppermute(odd, ax_name, [(h, (h + m) % side_arr) for h in range(side_arr)])
+        )
+    f_now = jnp.roll(
+        jnp.concatenate(stack_in[::-1], axis=0), (y2 + 1) * stack_in[0].shape[0], axis=0
+    )
+    return f_now
+
+
+follow_the_roads = functools.partial(proceed_islands, ax_name="req")
 
 
 def head_attention(query_matrix, prior_keys, prior_values, visible, scale_factor):
@@ -44,7 +64,7 @@
     source = jnp.where(is_live, source, 0)
     picked = jnp.take(row_block, source.reshape(-1), axis=0).reshape(groups, pair_slots, columns)
     outgoing = jnp.where(is_live[:, :, None], picked, jnp.zeros((), row_block.dtype))
-    arrived = lax.all_to_all(outgoing, "req", split_axis=0, concat_axis=0, tiled=True)
+    arrived = follow_the_roads(outgoing)
     own_shares = lax.dynamic_index_in_dim(shares, my_rank, 1, keepdims=False)
     own_starts = lax.dynamic_index_in_dim(starts, my_rank, 1, keepdims=False)
     within = jnp.arange(pair_slots, dtype=jnp.int32)[None, :]

time: 406 us -> 420 us (1.034)
  waiting for transfers between devices: 155 us -> 165 us
    all_to_all x1 -> x0, waiting for transfers between devices: 26.2 us -> none  [deal(): lax.all_to_all(outgoing, 'req', split_axis=0, concat_axis=0, tiled=True)]
    ppermute x0 -> x7, waiting for transfers between devices: none -> 21.5 us  [proceed_islands(): lax.ppermute(odd, ax_name, [(h, (h + m) % side_arr) for h in range(side_a...]
    reduce_scatter x1, waiting for transfers between devices: 128 us -> 144 us  [head_total(): lax.psum_scatter(partial_sum.astype(jnp.bfloat16), 'head', scatter_dimens...]
    ppermute x0 -> x7, starting transfers between devices: none -> 4.78 us  [proceed_islands(): lax.ppermute(odd, ax_name, [(h, (h + m) % side_arr) for h in range(side_a...]
    unnamed x40 -> x47, local copies, waits for them, and re-layouts: 9.63 us -> 11.1 us
  transfers between devices with their start and end apart: 3 -> 9, of which waited for: 2 -> 5; matrix products, arithmetic and copies ran while one was open for 44% -> 42% of each run, Pallas kernels for 0% -> 0%
where the time goes in v1:
time: 420 us; the launch traced here: 419 us
  waiting for transfers between devices  165 us (39%)
  matrix products  150 us (36%)
  local copies, waits for them, and re-layouts  61.2 us (15%)
  between operations  15.8 us (4%)
  other arithmetic  11.8 us (3%)
  blocking collectives  9.49 us (2%)
  starting transfers between devices  4.86 us (1%)
    reduce_scatter x1, waiting for transfers between devices, head_total(): lax.psum_scatter(partial_sum.astype(jnp.bfloat16), 'head', scatter_dimens...  144 us
    sub x16, matrix products, head_attention(): expo_terms = jnp.where(allowed, jnp.exp(scores - highest), 0.0)  74.2 us
    dot_general x16, matrix products, head_attention(): jnp.einsum('kts,skd->tkd', weights, prior_values, preferred_element_type=...  49.7 us
    dot_general x1, matrix products, project(): jnp.dot(row_block, lax.all_gather(out_weight, 'req', axis=1, tiled=True),...  25.9 us
    ppermute x7, waiting for transfers between devices, proceed_islands(): lax.ppermute(odd, ax_name, [(h, (h + m) % side_arr) for h in range(side_a...  21.5 us
    unnamed x47, local copies, waits for them, and re-layouts  11.1 us
    unnamed x1, blocking collectives  9.49 us
  transfers between devices with their start and end apart: 9, of which 5 were waited for; matrix products, arithmetic and copies ran while one was open for 42% of the time, Pallas kernels for 0%

profile of v1, /device:TPU:0, one launch (start us, length us, event | category | flops | bytes accessed | tf_op | source)
XLA Modules:
  0.0 418.7 jit_solution(16438353246714492377)
XLA Ops:
  13.1 9.5 %all-reduce.2 = (s32[16]{0:T(128)S(1)}, s32[8]{0:T(128)S(1)}) all-reduce(s32[16]{0:T(128)S(1)} %dynamic-update-slice, s32[8]{0:T(128)S(1)} %dynamic-update-slice.1), channel_id=1, replica_groups=mesh['req'=8,'head'=4] {'req'}, use_global_device_ids=true, to_apply=%add | all-reduce | flops 24 | bytes 192
  24.5 3.3 gather_fusion
  27.9 4.8 %gather_fusion.6 = s32[512]{0:T(512)S(1)} fusion(s32[2,14]{1,0:T(2,128)S(1)} %copy-done, s32[512]{0:T(512)S(1)} %bitcast.125), kind=kCustom, calls=%fused_computation.6 | custom fusion | bytes 8192 | tf_op jit(solution)/shard_map/jit(take_along_axis)/gather | solution.py:116
  33.3 5.5 %scatter_fusion = bf16[3584,256]{1,0:T(8,128)(2,1)} fusion(bf16[3584,256]{1,0:T(8,128)(2,1)} %bitcast.130, s32[512]{0:T(512)S(1)} %bitcast.143, bf16[512,256]{1,0:T(8,128)(2,1)S(1)} %copy-done.7), kind=kCustom, calls=%fused_computation.7 | custom fusion | bytes 788480 | tf_op jit(solution)/shard_map/scatter | solution.py:123
  38.8 3.1 gather_fusion.3
  41.9 3.6 scatter_fusion.1
  47.0 3.1 gather_fusion.1
  65.1 66.5 %while.21 = (s32[]{:T(128)}, bf16[8,256,2,128]{1,3,0,2:T(8,128)(2,1)S(1)}, s32[1,256]{1,0:T(1,128)S(1)}, bf16[8,256,2,128]{1,3,0,2:T(8,128)(2,1)}, bf16[1792,2,1...) while((s32[]{:T(128)}, bf16[8,256,2,128]{1,3,0,2:T(8,128)(2,1)S(1)}, ...), condition=%wide.region_13.14_spmd, body=%wide.region_10.13_spmd.sunk | while | flops 476710656 | bytes 11342941 | solution.py:143
  65.4 4.6 %fusion.96 = (f32[2,256]{1,0:T(2,128)S(1)}, f32[2,256,1792]{2,1,0:T(8,128)}) fusion(bf16[1792,2,128]{2,0,1:T(8,128)(2,1)S(1)} %get-tuple-element.261, pred[256,1792]{1,0:T(8,128)(4,1)S(1)} %iota_compare_fusion.6, bf16[8,256,2,128]{1,3,0,2:T(8,128)(2,1)} %get-tuple-element.260, s32[]{:T(128)S(6)} %copy.63), kind=kOutput, calls=%fused_computation.146.clone.1 | convolution fusion | flops 239470336 | bytes 5638148 | tf_op jit(solution)/shard_map/while/body/eval_jaxpr/sub | solution.py:40
  70.0 3.0 fusion.97
  73.5 4.6 %fusion.96 = (f32[2,256]{1,0:T(2,128)S(1)}, f32[2,256,1792]{2,1,0:T(8,128)}) fusion(bf16[1792,2,128]{2,0,1:T(8,128)(2,1)S(1)} %get-tuple-element.261, pred[256,1792]{1,0:T(8,128)(4,1)S(1)} %iota_compare_fusion.6, bf16[8,256,2,128]{1,3,0,2:T(8,128)(2,1)} %get-tuple-element.260, s32[]{:T(128)S(6)} %copy.63), kind=kOutput, calls=%fused_computation.146.clone.1 | convolution fusion | flops 239470336 | bytes 5638148 | tf_op jit(solution)/shard_map/while/body/eval_jaxpr/sub | solution.py:40
  78.1 4.4 %fusion.97 = bf16[1,256,2,128]{3,1,2,0:T(8,128)(2,1)S(1)} fusion(bf16[1792,2,128]{2,0,1:T(8,128)(2,1)} %get-tuple-element.262, f32[2,256,1792]{2,1,0:T(8,128)} %get-tuple-element.241, f32[2,256]{1,0:T(2,128)S(1)} %get-tuple-element.242), kind=kOutput, calls=%fused_computation.37.clone.1 | convolution fusion | flops 236781568 | bytes 4720640 | tf_op jit(solution)/shard_map/while/body/eval_jaxpr/kts,skd->tkd/dot_general | solution.py:42
  83.0 4.7 %fusion.96 = (f32[2,256]{1,0:T(2,128)S(1)}, f32[2,256,1792]{2,1,0:T(8,128)}) fusion(bf16[1792,2,128]{2,0,1:T(8,128)(2,1)S(1)} %get-tuple-element.261, pred[256,1792]{1,0:T(8,128)(4,1)S(1)} %iota_compare_fusion.6, bf16[8,256,2,128]{1,3,0,2:T(8,128)(2,1)} %get-tuple-element.260, s32[]{:T(128)S(6)} %copy.63), kind=kOutput, calls=%fused_computation.146.clone.1 | convolution fusion | flops 239470336 | bytes 5638148 | tf_op jit(solution)/shard_map/while/body/eval_jaxpr/sub | solution.py:40
  87.7 3.0 fusion.97
  91.2 4.6 %fusion.96 = (f32[2,256]{1,0:T(2,128)S(1)}, f32[2,256,1792]{2,1,0:T(8,128)}) fusion(bf16[1792,2,128]{2,0,1:T(8,128)(2,1)S(1)} %get-tuple-element.261, pred[256,1792]{1,0:T(8,128)(4,1)S(1)} %iota_compare_fusion.6, bf16[8,256,2,128]{1,3,0,2:T(8,128)(2,1)} %get-tuple-element.260, s32[]{:T(128)S(6)} %copy.63), kind=kOutput, calls=%fused_computation.146.clone.1 | convolution fusion | flops 239470336 | bytes 5638148 | tf_op jit(solution)/shard_map/while/body/eval_jaxpr/sub | solution.py:40
  95.8 3.0 fusion.97
  99.3 4.6 %fusion.96 = (f32[2,256]{1,0:T(2,128)S(1)}, f32[2,256,1792]{2,1,0:T(8,128)}) fusion(bf16[1792,2,128]{2,0,1:T(8,128)(2,1)S(1)} %get-tuple-element.261, pred[256,1792]{1,0:T(8,128)(4,1)S(1)} %iota_compare_fusion.6, bf16[8,256,2,128]{1,3,0,2:T(8,128)(2,1)} %get-tuple-element.260, s32[]{:T(128)S(6)} %copy.63), kind=kOutput, calls=%fused_computation.146.clone.1 | convolution fusion | flops 239470336 | bytes 5638148 | tf_op jit(solution)/shard_map/while/body/eval_jaxpr/sub | solution.py:40
  103.9 3.1 fusion.97
  107.5 4.6 %fusion.96 = (f32[2,256]{1,0:T(2,128)S(1)}, f32[2,256,1792]{2,1,0:T(8,128)}) fusion(bf16[1792,2,128]{2,0,1:T(8,128)(2,1)S(1)} %get-tuple-element.261, pred[256,1792]{1,0:T(8,128)(4,1)S(1)} %iota_compare_fusion.6, bf16[8,256,2,128]{1,3,0,2:T(8,128)(2,1)} %get-tuple-element.260, s32[]{:T(128)S(6)} %copy.63), kind=kOutput, calls=%fused_computation.146.clone.1 | convolution fusion | flops 239470336 | bytes 5638148 | tf_op jit(solution)/shard_map/while/body/eval_jaxpr/sub | solution.py:40
  112.2 3.0 fusion.97
  115.6 4.6 %fusion.96 = (f32[2,256]{1,0:T(2,128)S(1)}, f32[2,256,1792]{2,1,0:T(8,128)}) fusion(bf16[1792,2,128]{2,0,1:T(8,128)(2,1)S(1)} %get-tuple-element.261, pred[256,1792]{1,0:T(8,128)(4,1)S(1)} %iota_compare_fusion.6, bf16[8,256,2,128]{1,3,0,2:T(8,128)(2,1)} %get-tuple-element.260, s32[]{:T(128)S(6)} %copy.63), kind=kOutput, calls=%fused_computation.146.clone.1 | convolution fusion | flops 239470336 | bytes 5638148 | tf_op jit(solution)/shard_map/while/body/eval_jaxpr/sub | solution.py:40
  120.3 3.0 fusion.97
  123.8 4.6 %fusion.96 = (f32[2,256]{1,0:T(2,128)S(1)}, f32[2,256,1792]{2,1,0:T(8,128)}) fusion(bf16[1792,2,128]{2,0,1:T(8,128)(2,1)S(1)} %get-tuple-element.261, pred[256,1792]{1,0:T(8,128)(4,1)S(1)} %iota_compare_fusion.6, bf16[8,256,2,128]{1,3,0,2:T(8,128)(2,1)} %get-tuple-element.260, s32[]{:T(128)S(6)} %copy.63), kind=kOutput, calls=%fused_computation.146.clone.1 | convolution fusion | flops 239470336 | bytes 5638148 | tf_op jit(solution)/shard_map/while/body/eval_jaxpr/sub | solution.py:40
  128.4 3.0 fusion.97
  131.6 65.3 %while.20 = (s32[]{:T(128)}, bf16[8,256,2,128]{1,3,0,2:T(8,128)(2,1)S(1)}, s32[1,256]{1,0:T(1,128)S(1)}, bf16[8,256,2,128]{1,3,0,2:T(8,128)(2,1)}, bf16[1792,2,1...) while((s32[]{:T(128)}, bf16[8,256,2,128]{1,3,0,2:T(8,128)(2,1)S(1)}, ...), condition=%wide.region_9.10_spmd, body=%wide.region_6.9_spmd.sunk | while | flops 476710656 | bytes 11342941 | solution.py:143
  132.0 4.6 %fusion.91 = (f32[2,256]{1,0:T(2,128)S(1)}, f32[2,256,1792]{2,1,0:T(8,128)}) fusion(bf16[1792,2,128]{2,0,1:T(8,128)(2,1)S(1)} %get-tuple-element.282, pred[256,1792]{1,0:T(8,128)(4,1)S(1)} %iota_compare_fusion.5, bf16[8,256,2,128]{1,3,0,2:T(8,128)(2,1)} %get-tuple-element.281, s32[]{:T(128)S(6)} %copy.69), kind=kOutput, calls=%fused_computation.145.clone.1 | convolution fusion | flops 239470336 | bytes 5638148 | tf_op jit(solution)/shard_map/while/body/eval_jaxpr/sub | solution.py:40
  136.6 3.2 fusion.92
  140.3 4.6 %fusion.91 = (f32[2,256]{1,0:T(2,128)S(1)}, f32[2,256,1792]{2,1,0:T(8,128)}) fusion(bf16[1792,2,128]{2,0,1:T(8,128)(2,1)S(1)} %get-tuple-element.282, pred[256,1792]{1,0:T(8,128)(4,1)S(1)} %iota_compare_fusion.5, bf16[8,256,2,128]{1,3,0,2:T(8,128)(2,1)} %get-tuple-element.281, s32[]{:T(128)S(6)} %copy.69), kind=kOutput, calls=%fused_computation.145.clone.1 | convolution fusion | flops 239470336 | bytes 5638148 | tf_op jit(solution)/shard_map/while/body/eval_jaxpr/sub | solution.py:40
  144.9 3.0 fusion.92
  148.4 4.7 %fusion.91 = (f32[2,256]{1,0:T(2,128)S(1)}, f32[2,256,1792]{2,1,0:T(8,128)}) fusion(bf16[1792,2,128]{2,0,1:T(8,128)(2,1)S(1)} %get-tuple-element.282, pred[256,1792]{1,0:T(8,128)(4,1)S(1)} %iota_compare_fusion.5, bf16[8,256,2,128]{1,3,0,2:T(8,128)(2,1)} %get-tuple-element.281, s32[]{:T(128)S(6)} %copy.69), kind=kOutput, calls=%fused_computation.145.clone.1 | convolution fusion | flops 239470336 | bytes 5638148 | tf_op jit(solution)/shard_map/while/body/eval_jaxpr/sub | solution.py:40
  153.1 3.0 fusion.92
  156.6 4.6 %fusion.91 = (f32[2,256]{1,0:T(2,128)S(1)}, f32[2,256,1792]{2,1,0:T(8,128)}) fusion(bf16[1792,2,128]{2,0,1:T(8,128)(2,1)S(1)} %get-tuple-element.282, pred[256,1792]{1,0:T(8,128)(4,1)S(1)} %iota_compare_fusion.5, bf16[8,256,2,128]{1,3,0,2:T(8,128)(2,1)} %get-tuple-element.281, s32[]{:T(128)S(6)} %copy.69), kind=kOutput, calls=%fused_computation.145.clone.1 | convolution fusion | flops 239470336 | bytes 5638148 | tf_op jit(solution)/shard_map/while/body/eval_jaxpr/sub | solution.py:40
  161.2 3.0 fusion.92
  164.7 4.6 %fusion.91 = (f32[2,256]{1,0:T(2,128)S(1)}, f32[2,256,1792]{2,1,0:T(8,128)}) fusion(bf16[1792,2,128]{2,0,1:T(8,128)(2,1)S(1)} %get-tuple-element.282, pred[256,1792]{1,0:T(8,128)(4,1)S(1)} %iota_compare_fusion.5, bf16[8,256,2,128]{1,3,0,2:T(8,128)(2,1)} %get-tuple-element.281, s32[]{:T(128)S(6)} %copy.69), kind=kOutput, calls=%fused_computation.145.clone.1 | convolution fusion | flops 239470336 | bytes 5638148 | tf_op jit(solution)/shard_map/while/body/eval_jaxpr/sub | solution.py:40
  169.3 3.2 fusion.92
  173.0 4.6 %fusion.91 = (f32[2,256]{1,0:T(2,128)S(1)}, f32[2,256,1792]{2,1,0:T(8,128)}) fusion(bf16[1792,2,128]{2,0,1:T(8,128)(2,1)S(1)} %get-tuple-element.282, pred[256,1792]{1,0:T(8,128)(4,1)S(1)} %iota_compare_fusion.5, bf16[8,256,2,128]{1,3,0,2:T(8,128)(2,1)} %get-tuple-element.281, s32[]{:T(128)S(6)} %copy.69), kind=kOutput, calls=%fused_computation.145.clone.1 | convolution fusion | flops 239470336 | bytes 5638148 | tf_op jit(solution)/shard_map/while/body/eval_jaxpr/sub | solution.py:40
  177.6 3.0 fusion.92
  181.1 4.6 %fusion.91 = (f32[2,256]{1,0:T(2,128)S(1)}, f32[2,256,1792]{2,1,0:T(8,128)}) fusion(bf16[1792,2,128]{2,0,1:T(8,128)(2,1)S(1)} %get-tuple-element.282, pred[256,1792]{1,0:T(8,128)(4,1)S(1)} %iota_compare_fusion.5, bf16[8,256,2,128]{1,3,0,2:T(8,128)(2,1)} %get-tuple-element.281, s32[]{:T(128)S(6)} %copy.69), kind=kOutput, calls=%fused_computation.145.clone.1 | convolution fusion | flops 239470336 | bytes 5638148 | tf_op jit(solution)/shard_map/while/body/eval_jaxpr/sub | solution.py:40
  185.7 3.0 fusion.92
  189.2 4.6 %fusion.91 = (f32[2,256]{1,0:T(2,128)S(1)}, f32[2,256,1792]{2,1,0:T(8,128)}) fusion(bf16[1792,2,128]{2,0,1:T(8,128)(2,1)S(1)} %get-tuple-element.282, pred[256,1792]{1,0:T(8,128)(4,1)S(1)} %iota_compare_fusion.5, bf16[8,256,2,128]{1,3,0,2:T(8,128)(2,1)} %get-tuple-element.281, s32[]{:T(128)S(6)} %copy.69), kind=kOutput, calls=%fused_computation.145.clone.1 | convolution fusion | flops 239470336 | bytes 5638148 | tf_op jit(solution)/shard_map/while/body/eval_jaxpr/sub | solution.py:40
  193.8 3.0 fusion.92
  197.0 25.9 %convolution_convert_fusion = bf16[512,8192]{1,0:T(8,128)(2,1)} fusion(bf16[2048,8192]{1,0:T(8,128)(2,1)} %all-gather.2.cloned.1.call-done, bf16[256,2048]{0,1:T(8,128)(2,1)S(1)} %bitcast.138, bf16[256,2048]{0,1:T(8,128)(2,1)S(1)} %bitcast.139), kind=kOutput, calls=%fused_computation.48 | convolution fusion | flops 17188257792 | bytes 44040192 | tf_op jit(solution)/shard_map/dot_general | solution.py:77
  223.9 143.6 %reduce-scatter.2.cloned.1.call-done = bf16[512,2048]{1,0:T(8,128)(2,1)} async-done(((bf16[512,8192]{1,0:T(8,128)(2,1)}), bf16[512,2048]{1,0:T(8,128)(2,1)}) %reduce-scatter.2.cloned.1.call-update) | async-done | bytes 2097168 | tf_op jit(solution)/shard_map/reduce_scatter | solution.py:85
  367.5 6.5 %gather_fusion.5 = bf16[512,2048]{1,0:T(8,128)(2,1)S(1)} fusion(bf16[512,2048]{1,0:T(8,128)(2,1)} %reduce-scatter.2.cloned.1.call-done, s32[1024]{0:T(1024)S(1)} %pad_clamp_fusion), kind=kCustom, calls=%fused_computation.5 | custom fusion | bytes 4196352 | tf_op jit(solution)/shard_map/jit(_take)/gather | solution.py:65
  380.7 3.3 collective-permute-done
  385.3 5.1 %collective-permute-done.1 = bf16[1,64,2048]{2,1,0:T(8,128)(2,1)} collective-permute-done((bf16[1,64,2048]{2,1,0:T(8,128)(2,1)}, bf16[1,64,2048]{2,1,0:T(8,128)(2,1)}, u32[]{:S(2)}, u32[]{:S(2)}) %collective-permute-start.1) | collective-permute-done | bytes 262176 | tf_op jit(solution)/shard_map/ppermute | solution.py:20
  391.4 12.8 %collective-permute-done.3 = bf16[1,64,2048]{2,1,0:T(8,128)(2,1)S(1)} collective-permute-done((bf16[1,64,2048]{2,1,0:T(8,128)(2,1)S(1)}, bf16[1,64,2048]{2,1,0:T(8,128)(2,1)S(1)}, u32[]{:S(2)}, u32[]{:S(2)}) %collective-permute-start.3) | collective-permute-done | bytes 262176 | tf_op jit(solution)/shard_map/ppermute | solution.py:20
  405.4 3.8 scatter_custom_fusion.2
  (161 shorter events, 44.6 us)
Async XLA Ops:
  7.2 189.8 %all-gather.2.cloned.1.call-start = ((), (), s32[]{:S(2)}) async-start(), calls=%async_computation.1 | async-start | bytes 37748736 | tf_op jit(solution)/shard_map/all_gather | solution.py:79
  10.1 0.7 copy-start.11
  10.1 2.0 copy-start.10
  10.1 14.0 %copy-start.9 = (s32[2]{0:T(128)S(1)}, s32[2]{0:T(128)}, u32[]{:S(2)}) copy-start(s32[2]{0:T(128)} %param.24) | copy-start | bytes 28
  10.2 357.4 %reduce-scatter.2.cloned.1.call-start = ((), (), s32[]{:S(2)}) async-start(), calls=%async_computation.2 | async-start | bytes 10485760 | tf_op jit(solution)/shard_map/reduce_scatter | solution.py:85
  24.5 3.4 copy-start
  27.9 5.4 %copy-start.7 = (bf16[512,256]{1,0:T(8,128)(2,1)S(1)}, bf16[512,256]{1,0:T(8,128)(2,1)}, u32[]{:S(2)}) copy-start(bf16[512,256]{1,0:T(8,128)(2,1)} %param.18) | copy-start | bytes 786436
  33.2 8.6 %copy-start.2 = (bf16[28,128,256]{2,1,0:T(8,128)(2,1)S(1)}, bf16[28,128,256]{2,1,0:T(8,128)(2,1)}, u32[]{:S(2)}) copy-start(bf16[28,128,256]{2,1,0:T(8,128)(2,1)} %param.21) | copy-start | bytes 5505028
  33.3 8.6 %copy-start.8 = (bf16[512,256]{1,0:T(8,128)(2,1)S(1)}, bf16[512,256]{1,0:T(8,128)(2,1)}, u32[]{:S(2)}) copy-start(bf16[512,256]{1,0:T(8,128)(2,1)} %param.19) | copy-start | bytes 786436
  45.4 6.2 %copy-start.1 = (bf16[3584,256]{1,0:T(8,128)(2,1)}, bf16[3584,256]{1,0:T(8,128)(2,1)S(1)}, u32[]{:S(2)}) copy-start(bf16[3584,256]{1,0:T(8,128)(2,1)S(1)} %scatter_fusion.1) | copy-start | bytes 5505028
  54.3 2.4 copy-start.4
  56.9 1.5 copy-start.5
  60.9 2.4 copy-start.3
  63.6 1.5 copy-start.6
  376.1 7.8 %collective-permute-start = (bf16[1,64,2048]{2,1,0:T(8,128)(2,1)}, bf16[1,64,2048]{2,1,0:T(8,128)(2,1)}, u32[]{:S(2)}, u32[]{:S(2)}) collective-permute-start(bf16[1,64,2048]{2,1,0:T(8,128)(2,1)} %get-tuple-element.142), channel_id=1, source_target_pairs={{0,28},{4,0},{8,4},{12,8},{16,12},{20,16},{24,20},{28,24},{1,29},{... | collective-permute-start | bytes 786440 | tf_op jit(solution)/shard_map/ppermute | solution.py:20
  377.7 12.7 %collective-permute-start.1 = (bf16[1,64,2048]{2,1,0:T(8,128)(2,1)}, bf16[1,64,2048]{2,1,0:T(8,128)(2,1)}, u32[]{:S(2)}, u32[]{:S(2)}) collective-permute-start(bf16[1,64,2048]{2,1,0:T(8,128)(2,1)} %get-tuple-element.141), channel_id=1, source_target_pairs={{0,24},{4,28},{8,0},{12,4},{16,8},{20,12},{24,16},{28,20},{1,25},{... | collective-permute-start | bytes 786440 | tf_op jit(solution)/shard_map/ppermute | solution.py:20
  378.7 12.7 %collective-permute-start.2 = (bf16[1,64,2048]{2,1,0:T(8,128)(2,1)S(1)}, bf16[1,64,2048]{2,1,0:T(8,128)(2,1)S(1)}, u32[]{:S(2)}, u32[]{:S(2)}) collective-permute-start(bf16[1,64,2048]{2,1,0:T(8,128)(2,1)S(1)} %get-tuple-element.140), channel_id=1, source_target_pairs={{0,20},{4,24},{8,28},{12,0},{16,4},{20,8},{24,12},{28,16},{1,21},{... | collective-permute-start | bytes 786440 | tf_op jit(solution)/shard_map/ppermute | solution.py:20
  379.0 25.1 %collective-permute-start.3 = (bf16[1,64,2048]{2,1,0:T(8,128)(2,1)S(1)}, bf16[1,64,2048]{2,1,0:T(8,128)(2,1)S(1)}, u32[]{:S(2)}, u32[]{:S(2)}) collective-permute-start(bf16[1,64,2048]{2,1,0:T(8,128)(2,1)S(1)} %get-tuple-element.139), channel_id=1, source_target_pairs={{0,16},{4,20},{8,24},{12,28},{16,0},{20,4},{24,8},{28,12},{1,17},{... | collective-permute-start | bytes 786440 | tf_op jit(solution)/shard_map/ppermute | solution.py:20
  380.5 24.0 %collective-permute-start.4 = (bf16[1,64,2048]{2,1,0:T(8,128)(2,1)S(1)}, bf16[1,64,2048]{2,1,0:T(8,128)(2,1)S(1)}, u32[]{:S(2)}, u32[]{:S(2)}) collective-permute-start(bf16[1,64,2048]{2,1,0:T(8,128)(2,1)S(1)} %get-tuple-element.138), channel_id=1, source_target_pairs={{0,12},{4,16},{8,20},{12,24},{16,28},{20,0},{24,4},{28,8},{1,13},{... | collective-permute-start | bytes 786440 | tf_op jit(solution)/shard_map/ppermute | solution.py:20
  384.0 20.6 %collective-permute-start.5 = (bf16[1,64,2048]{2,1,0:T(8,128)(2,1)S(1)}, bf16[1,64,2048]{2,1,0:T(8,128)(2,1)S(1)}, u32[]{:S(2)}, u32[]{:S(2)}) collective-permute-start(bf16[1,64,2048]{2,1,0:T(8,128)(2,1)S(1)} %get-tuple-element.137), channel_id=1, source_target_pairs={{0,8},{4,12},{8,16},{12,20},{16,24},{20,28},{24,0},{28,4},{1,9},{5... | collective-permute-start | bytes 786440 | tf_op jit(solution)/shard_map/ppermute | solution.py:20
  390.4 14.2 %collective-permute-start.6 = (bf16[1,64,2048]{2,1,0:T(8,128)(2,1)S(1)}, bf16[1,64,2048]{2,1,0:T(8,128)(2,1)S(1)}, u32[]{:S(2)}, u32[]{:S(2)}) collective-permute-start(bf16[1,64,2048]{2,1,0:T(8,128)(2,1)S(1)} %get-tuple-element.136), channel_id=1, source_target_pairs={{0,4},{4,8},{8,12},{12,16},{16,20},{20,24},{24,28},{28,0},{1,5},{5... | collective-permute-start | bytes 786440 | tf_op jit(solution)/shard_map/ppermute | solution.py:20
Sparse Core Ops, SparseCore 0:
  10.3 163.3 all-gather.1
  223.1 144.3 reduce-scatter.1
